TPU v7x, 32 devices: a whole 2x2x4 slice. The times are simulated.
32 devices in a mesh: tile: 8 (over y, x, core), mem: 4 (over z).
Axes of the slice: x: 2, y: 2, z: 4, core: 2. Of those that a mesh axis runs over, the one named last changes fastest.
Arguments:
- control: bfloat16 [80, 1, 360, 720], P('mem', None, 'tile'), may hold values from -6 to 6
- perturb: bfloat16 [80, 1, 360, 720], P('mem', None, 'tile'), may hold values from -6 to 6
- lon_taps: bfloat16 [17], replicated, may hold values from 0.026367188 to 0.07910156
- lat_taps: bfloat16 [17], replicated, may hold values from 0.026367188 to 0.07910156
- innov: float32 [8, 8, 256], P('tile'), may hold values from -6 to 6
- inv_var: float32 [8, 8, 256], P('tile'), may hold values from 1 to 8
- cell_index: int32 [8, 8, 256], P('tile'), may hold values from 0 to 32399, as said below
- counts: int32 [8, 8], P('tile'), may hold values from 0 to 256, as said below
Outputs:
- gradient: float32 [80, 1, 360, 720], P('mem', None, 'tile')
Inputs may be any that keep to these rules, and one draw needn't show every extreme that they name: `cell_index`: an observation's cell within its owning tile, level * 45 * 720 + longitude within the tile * 720 + latitude; both ends are taken. `counts`: live slots per pair of tiles; some pair fills all 256 slots in every draw, and some owning tiles receive far more than others.
All inputs are finite; a program needn't handle non-finite values.
Results may differ from a plain program's by a relative error of at most 0.00066.
Values may be sent and summed in bfloat16 or wider, within the bound.
No kernel may reach another device: no remote copies, remote signals or barrier semaphores. Data moves between devices by JAX's collectives and lax.ppermute only.
A program may use at most 64 MiB of HBM per device.

v0:
```python
import math
import jax
import jax.numpy as jnp
from jax import lax
from jax.sharding import PartitionSpec as P


def extended_2(block, sides, width):
    for axis, dim in sides:
        count = lax.axis_size(axis)
        forward = [(i, i + 1) for i in range(count - 1)]
        forward.append((count - 1, 0))
        backward = [(target, source) for source, target in forward]
        low = lax.ppermute(
            lax.slice_in_dim(block, block.shape[dim] - width, None, axis=dim), axis, forward
        )
        high = lax.ppermute(lax.slice_in_dim(block, 0, width, axis=dim), axis, backward)
        block = jnp.concatenate([low, block, high], axis=dim)
    return block


def band_from(offsets, tap_weights):
    radius = tap_weights.shape[0] - 1
    taps = tap_weights.astype(jnp.float32)
    band = jnp.zeros(offsets.shape, jnp.float32)
    for offset in range(radius + 1):
        band = band + jnp.where(offsets == offset, taps[offset], 0.0)
    return band.astype(jnp.bfloat16)


def lon_band(tap_weights, lon_cells):
    radius = tap_weights.shape[0] - 1
    row_ids = lax.broadcasted_iota(jnp.int32, (lon_cells, lon_cells + 2 * radius), 0)
    col_ids = lax.broadcasted_iota(jnp.int32, (lon_cells, lon_cells + 2 * radius), 1)
    return band_from(jnp.abs(col_ids - row_ids - radius), tap_weights)


def lat_block_band(tap_weights, block_cells):
    radius = tap_weights.shape[0] - 1
    row_ids = lax.broadcasted_iota(jnp.int32, (block_cells + 2 * radius, block_cells), 0)
    col_ids = lax.broadcasted_iota(jnp.int32, (block_cells + 2 * radius, block_cells), 1)
    return band_from(jnp.abs(row_ids - radius - col_ids), tap_weights)


def localize(extended, band_lon, band_blocks, radius, block_cells):
    along = jnp.einsum(
        "ij,mljk->mlik", band_lon, extended, preferred_element_type=jnp.float32
    ).astype(jnp.bfloat16)
    members_here, levels, lon_cells, lat_cells = along.shape
    padded = jnp.pad(along, ((0, 0), (0, 0), (0, 0), (radius, radius)))
    block_count = lat_cells // block_cells
    windows = jnp.stack(
        [
            padded[:, :, :, block * block_cells : block * block_cells + block_cells + 2 * radius]
            for block in range(block_count)
        ],
        axis=3,
    )
    result = jnp.einsum("mlibk,kq->mlibq", windows, band_blocks, preferred_element_type=jnp.float32)
    return result.reshape(members_here, levels, lon_cells, lat_cells)


def pick_cells(field_rows, row_index, col_index, block_rows):
    row_count, col_count = field_rows.shape
    field_cols = field_rows.T

    def pick_one_block(indices):
        rows_here, cols_here = indices
        onehot_rows = (
            rows_here[:, None] == jnp.arange(row_count, dtype=jnp.int32)[None, :]
        ).astype(jnp.float32)
        onehot_cols = (
            cols_here[:, None] == jnp.arange(col_count, dtype=jnp.int32)[None, :]
        ).astype(jnp.float32)
        picked = jnp.dot(
            onehot_cols,
            field_cols,
            precision=lax.Precision.HIGHEST,
            preferred_element_type=jnp.float32,
        )
        return jnp.sum(picked * onehot_rows, axis=1)

    values = lax.map(
        pick_one_block, (row_index.reshape(-1, block_rows), col_index.reshape(-1, block_rows))
    )
    return values.reshape(-1)


def spread_cells(misfit, row_index, col_index, row_count, col_count, block_rows):

    def spread_one_block(total, items):
        rows_here, cols_here, values = items
        onehot_rows = (
            rows_here[:, None] == jnp.arange(row_count, dtype=jnp.int32)[None, :]
        ).astype(jnp.float32)
        onehot_cols = (
            cols_here[:, None] == jnp.arange(col_count, dtype=jnp.int32)[None, :]
        ).astype(jnp.float32)
        weighted = onehot_rows * values[:, None]
        return (
            total
            + jnp.dot(
                weighted.T,
                onehot_cols,
                precision=lax.Precision.HIGHEST,
                preferred_element_type=jnp.float32,
            ),
            None,
        )

    start = jnp.zeros((row_count, col_count), jnp.float32)
    items = (
        row_index.reshape(-1, block_rows),
        col_index.reshape(-1, block_rows),
        misfit.reshape(-1, block_rows),
    )
    total, _ = lax.scan(spread_one_block, start, items)
    return total


def local(control, perturb, lon_taps, lat_taps, innov, inv_var, cell_index, counts):
    members_here, levels, lon_cells, lat_cells = control.shape
    radius = lon_taps.shape[0] - 1
    block_cells = 144
    band_lon = lon_band(lon_taps, lon_cells)
    band_blocks = lat_block_band(lat_taps, block_cells)
    extended = extended_2(control, (("tile", 2),), radius)
    smoothed = localize(extended, band_lon, band_blocks, radius, block_cells)
    member_sum = jnp.sum(perturb.astype(jnp.float32) * smoothed, axis=0)
    slot_ids = lax.broadcasted_iota(jnp.int32, innov.shape, 2)
    is_live = slot_ids < counts[:, :, None]
    weights = jnp.where(is_live, inv_var, 0.0)
    received = (
        lax.all_to_all(innov, "tile", split_axis=1, concat_axis=0, tiled=True),
        lax.all_to_all(weights, "tile", split_axis=1, concat_axis=0, tiled=True),
        lax.all_to_all(cell_index, "tile", split_axis=1, concat_axis=0, tiled=True),
    )
    observed = received[0].reshape(-1)
    weight_recv = received[1].reshape(-1)
    cells_hit = received[2].reshape(-1)
    row_index = cells_hit // lat_cells
    col_index = cells_hit % lat_cells
    row_count = levels * lon_cells
    block_rows = math.gcd(observed.shape[0], 1024)
    increment = lax.psum(member_sum, "mem")
    at_cells = pick_cells(increment.reshape(row_count, lat_cells), row_index, col_index, block_rows)
    misfit = weight_recv * (at_cells - observed)
    spread = spread_cells(misfit, row_index, col_index, row_count, lat_cells, block_rows)
    spread = spread.reshape(levels, lon_cells, lat_cells)
    wide_pert = extended_2(perturb, (("tile", 2),), radius)
    wide_spread = extended_2(spread, (("tile", 1),), radius)
    wide_products = (wide_pert.astype(jnp.float32) * wide_spread[None]).astype(jnp.bfloat16)
    return control.astype(jnp.float32) + localize(
        wide_products, band_lon, band_blocks, radius, block_cells
    )


def solution(mesh):
    return jax.shard_map(
        local,
        mesh=mesh,
        in_specs=(
            P("mem", None, "tile", None),
            P("mem", None, "tile", None),
            P(),
            P(),
            P("tile", None, None),
            P("tile", None, None),
            P("tile", None, None),
            P("tile", None),
        ),
        out_specs=P("mem", None, "tile", None),
        check_vma=False,
    )
```

profile of v0, /device:TPU:11, one launch (start us, length us, event | category | flops | bytes accessed | tf_op | source)
XLA Modules:
  0.0 176.9 jit_solution(8008073635435257452)
XLA Ops:
  6.6 1.5 fusion.166
  8.1 1.8 %collective-permute-start.2 = (bf16[20,1,16,720]{3,2,0,1:T(8,128)(2,1)S(1)}, bf16[20,1,16,720]{3,2,0,1:T(8,128)(2,1)}, u32[]{:S(2)}, u32[]{:S(2)}) collective-permute-start(bf16[20,1,16,720]{3,2,0,1:T(8,128)(2,1)S(1)} %get-tuple-element.115), channel_id=1, source_target_pairs={{0,4},{4,8},{8,12},{12,16},{16,20},{20,24},{24,28},{28,0},{1,5},{5... | collective-permute-start | bytes 1382408 | tf_op jit(solution)/shard_map/ppermute | solution.py:14
  9.9 1.3 copy.48
  11.2 4.9 %all-to-all-start = ((s32[1,8,256]{2,0,1:T(1,128)}), s32[1,8,256]{2,0,1:T(1,128)S(1)}, u32[]{:S(2)}, u32[]{:S(2)}) async-start(s32[1,8,256]{2,0,1:T(1,128)} %copy.48), calls=%async_computation | async-start | bytes 16384 | tf_op jit(solution)/shard_map/all_to_all | solution.py:136
  16.1 2.2 %fusion.167 = (bf16[20,1,16,720]{3,2,0,1:T(8,128)(2,1)}, bf16[20,1,16,720]{3,2,0,1:T(8,128)(2,1)S(1)}) fusion(bf16[20,1,45,720]{3,2,0,1:T(8,128)(2,1)} %bitcast.147), kind=kLoop, calls=%fused_computation.200 | loop fusion | bytes 1843200 | tf_op jit(solution)/shard_map/slice | solution.py:15
  18.3 1.5 collective-permute-start
  23.2 4.4 %all-to-all-start.1 = ((f32[1,8,256]{2,0,1:T(1,128)}), f32[1,8,256]{2,0,1:T(1,128)S(1)}, u32[]{:S(2)}, u32[]{:S(2)}) async-start(f32[1,8,256]{2,0,1:T(1,128)} %compare_select_fusion), calls=%async_computation.1 | async-start | bytes 16384 | tf_op jit(solution)/shard_map/all_to_all | solution.py:135
  27.7 5.6 %all-to-all-done.1 = f32[1,8,256]{2,0,1:T(1,128)S(1)} async-done(((f32[1,8,256]{2,0,1:T(1,128)}), f32[1,8,256]{2,0,1:T(1,128)S(1)}, u32[]{:S(2)}, u32[]{:S(2)}) %all-to-all-start.1) | async-done | bytes 8224 | tf_op jit(solution)/shard_map/all_to_all | solution.py:135
  33.4 4.0 %all-to-all-start.2 = ((f32[1,8,256]{2,0,1:T(1,128)}), f32[1,8,256]{2,0,1:T(1,128)S(1)}, u32[]{:S(2)}, u32[]{:S(2)}) async-start(f32[1,8,256]{2,0,1:T(1,128)} %copy.57), calls=%async_computation.2 | async-start | bytes 16384 | tf_op jit(solution)/shard_map/all_to_all | solution.py:134
  37.5 3.1 %all-to-all-done.2 = f32[1,8,256]{2,0,1:T(1,128)S(1)} async-done(((f32[1,8,256]{2,0,1:T(1,128)}), f32[1,8,256]{2,0,1:T(1,128)S(1)}, u32[]{:S(2)}, u32[]{:S(2)}) %all-to-all-start.2) | async-done | bytes 8224 | tf_op jit(solution)/shard_map/all_to_all | solution.py:134
  40.7 12.1 %fusion.31 = bf16[20,1,45,720]{3,2,0,1:T(8,128)(2,1)S(1)} fusion(bf16[20,1,16,720]{3,2,0,1:T(8,128)(2,1)} %collective-permute-done.3, bf16[20,1,45,720]{3,2,0,1:T(8,128)(2,1)S(1)} %bitcast.146, bf16[20,1,16,720]{3,2,0,1:T(8,128)(2,1)} %collective-permute-done.2, f32[]{:T(128)} %bitcast.31, f32[]{:T(128)} %bitcast.30, f32[]{:T(128)} %bitcast.29, ...), kind=kOutput, calls=%fused_computation.44 | convolution fusion | flops 107279912 | bytes 3513668 | tf_op jit(solution)/shard_map/ij,mljk->mlik/dot_general | solution.py:46
  53.7 11.5 %fusion.25 = f32[20,45,5,144]{3,1,2,0:T(8,128)S(1)} fusion(f32[]{:T(128)} %bitcast.58, f32[]{:T(128)} %bitcast.57, f32[]{:T(128)} %bitcast.56, f32[]{:T(128)} %bitcast.55, f32[]{:T(128)} %bitcast.54, f32[]{:T(128)} %bitcast.53, f32[]{:T(128)} %bitcast.52, f32[]{:T(128)} %bitcast.51, f32[]{:T(128)} %bitcast.50, f32[]{:T(128)} %bitcast.49, f32[]{:T(128)} %bitcast.48, ...), kind=kOutput, calls=%fused_computation.38 | convolution fusion | flops 229439232 | bytes 4176772 | tf_op jit(solution)/shard_map/mlibk,kq->mlibq/dot_general | solution.py:59
  65.2 6.4 %copy.55 = f32[20,45,5,144]{3,2,1,0:T(8,128)} copy(f32[20,45,5,144]{3,1,2,0:T(8,128)S(1)} %fusion.25) | data formatting | bytes 5184000 | tf_op jit(solution)/shard_map/mlibk,kq->mlibq/dot_general | solution.py:59
  71.6 4.9 %reshape.136 = f32[20,1,45,720]{3,2,0,1:T(8,128)S(1)} reshape(f32[20,45,5,144]{3,2,1,0:T(8,128)} %copy.55) | data formatting | bytes 5184000 | tf_op jit(solution)/shard_map/reshape | solution.py:60
  76.4 2.4 %multiply_reduce_fusion = f32[45,720]{1,0:T(8,128)} fusion(f32[20,1,45,720]{3,2,0,1:T(8,128)S(1)} %reshape.136, bf16[20,1,45,720]{3,2,1,0:T(8,128)(2,1)} %param.13), kind=kLoop, calls=%fused_computation.22 | loop fusion | flops 1911600 | bytes 4017600 | tf_op jit(solution)/shard_map/reduce_sum | solution.py:129
  78.9 32.7 %all-reduce.4.cloned.1.call-done = f32[720,45]{0,1:T(8,128)} async-done(((f32[720,45]{0,1:T(8,128)}), f32[720,45]{0,1:T(8,128)}) %all-reduce.4.cloned.1.call-update) | async-done | bytes 129616 | tf_op jit(solution)/shard_map/psum | solution.py:145
  111.6 1.1 copy.56
  112.7 3.8 %while.21 = (s32[]{:T(128)}, f32[2,1024]{1,0:T(2,128)S(1)}, s32[2,1024]{1,0:T(2,128)S(1)}, s32[2,1024]{1,0:T(2,128)S(1)}, f32[720,45]{1,0:T(8,128)S(1)}, /*index=5*/s32[]{:T(128)}, s32[]{:T(128)}) while((s32[]{:T(128)}, f32[2,1024]{1,0:T(2,128)S(1)}, s32[2,1024]{1,0:T(2,128)S(1)}, s32[2,1024]{1,0:T(2,128)S(1)}, f32[720,45]{1,0:T(8,128)S(1)}, ...), condition=%wide.region_4.5_spmd, body=%wide.region_2.4_spmd.sunk | while | flops 399005696 | bytes 166549 | solution.py:83
  112.7 1.8 %fusion.179 = f32[1024]{0:T(1024)S(1)} fusion(f32[720,45]{1,0:T(8,128)S(1)} %get-tuple-element.245, s32[1024]{0:T(1024)S(1)} %bitcast.156, s32[1024]{0:T(1024)S(1)} %bitcast.157), kind=kOutput, calls=%fused_computation.4.clone.1 | convolution fusion | flops 399005696 | bytes 141888 | tf_op jit(solution)/shard_map/while/body/eval_jaxpr/dot_general | solution.py:75
  114.6 1.8 %fusion.179 = f32[1024]{0:T(1024)S(1)} fusion(f32[720,45]{1,0:T(8,128)S(1)} %get-tuple-element.245, s32[1024]{0:T(1024)S(1)} %bitcast.156, s32[1024]{0:T(1024)S(1)} %bitcast.157), kind=kOutput, calls=%fused_computation.4.clone.1 | convolution fusion | flops 399005696 | bytes 141888 | tf_op jit(solution)/shard_map/while/body/eval_jaxpr/dot_general | solution.py:75
  116.5 3.1 %while.22 = (s32[]{:T(128)}, f32[45,720]{1,0:T(8,128)S(1)}, s32[2,1024]{1,0:T(2,128)S(1)}, f32[2,1024]{1,0:T(2,128)S(1)}, s32[2,1024]{1,0:T(2,128)S(1)}, /*index=5*/s32[]{:T(128)}, s32[]{:T(128)}) while((s32[]{:T(128)}, f32[45,720]{1,0:T(8,128)S(1)}, s32[2,1024]{1,0:T(2,128)S(1)}, f32[2,1024]{1,0:T(2,128)S(1)}, ...), condition=%wide.region_6.7_spmd.clone, body=%wide.region_5.6_spmd.clone.sunk | while | flops 399025440 | bytes 296159 | solution.py:117
  116.6 1.5 fusion.181
  118.1 1.5 fusion.181
  119.7 3.9 %collective-permute-start.4 = (f32[1,16,720]{2,1,0:T(8,128)S(1)}, f32[1,16,720]{2,1,0:T(8,128)S(1)}, u32[]{:S(2)}, u32[]{:S(2)}) collective-permute-start(f32[1,16,720]{2,1,0:T(8,128)S(1)} %get-tuple-element.119), channel_id=1, source_target_pairs={{0,4},{4,8},{8,12},{12,16},{16,20},{20,24},{24,28},{28,0},{1,5},{5... | collective-permute-start | bytes 138248 | tf_op jit(solution)/shard_map/ppermute | solution.py:14
  123.6 1.2 collective-permute-done.4
  124.7 3.2 %collective-permute-done.5 = f32[1,16,720]{2,1,0:T(8,128)S(1)} collective-permute-done((f32[1,16,720]{2,1,0:T(8,128)S(1)}, f32[1,16,720]{2,1,0:T(8,128)S(1)}, u32[]{:S(2)}, u32[]{:S(2)}) %collective-permute-start.5) | collective-permute-done | bytes 46112 | tf_op jit(solution)/shard_map/ppermute | solution.py:17
  128.0 12.3 %fusion.30 = bf16[20,1,45,720]{3,2,0,1:T(8,128)(2,1)S(1)} fusion(bf16[20,16,720]{2,1,0:T(8,128)(2,1)} %bitcast.8, bf16[20,45,720]{2,1,0:T(8,128)(2,1)S(1)} %bitcast.148, bf16[20,16,720]{2,1,0:T(8,128)(2,1)} %bitcast.5, f32[77,720]{1,0:T(8,128)S(1)} %maximum_bitcast_fusion.6, f32[]{:T(128)} %bitcast.31, f32[]{:T(128)} %bitcast.30, f32[]{:T(128)} %bitcast.29, ...), kind=kOutput, calls=%fused_computation.43 | convolution fusion | flops 109497512 | bytes 3735428 | tf_op jit(solution)/shard_map/ij,mljk->mlik/dot_general | solution.py:46
  141.2 11.5 %fusion.23 = f32[20,45,5,144]{3,1,2,0:T(8,128)S(1)} fusion(f32[]{:T(128)} %bitcast.58, f32[]{:T(128)} %bitcast.57, f32[]{:T(128)} %bitcast.56, f32[]{:T(128)} %bitcast.55, f32[]{:T(128)} %bitcast.54, f32[]{:T(128)} %bitcast.53, f32[]{:T(128)} %bitcast.52, f32[]{:T(128)} %bitcast.51, f32[]{:T(128)} %bitcast.50, f32[]{:T(128)} %bitcast.49, f32[]{:T(128)} %bitcast.48, ...), kind=kOutput, calls=%fused_computation.36 | convolution fusion | flops 229439232 | bytes 4176772 | tf_op jit(solution)/shard_map/mlibk,kq->mlibq/dot_general | solution.py:59
  152.7 6.4 %copy.59 = f32[20,45,5,144]{3,2,1,0:T(8,128)} copy(f32[20,45,5,144]{3,1,2,0:T(8,128)S(1)} %fusion.23) | data formatting | bytes 5184000 | tf_op jit(solution)/shard_map/mlibk,kq->mlibq/dot_general | solution.py:59
  159.1 4.9 %reshape.141 = f32[20,1,45,720]{3,2,0,1:T(8,128)S(1)} reshape(f32[20,45,5,144]{3,2,1,0:T(8,128)} %copy.59) | data formatting | bytes 5184000 | tf_op jit(solution)/shard_map/reshape | solution.py:60
  164.0 1.7 convert_add_fusion
  165.7 4.4 %copy.60 = f32[20,1,45,720]{3,1,2,0:T(1,128)} copy(f32[20,1,45,720]{3,2,0,1:T(8,128)S(1)} %convert_add_fusion) | data formatting | bytes 5184000 | tf_op jit(solution)/shard_map/add | solution.py:153
  (64 shorter events, 5.7 us)
Async XLA Ops:
  6.5 34.1 %copy-start = (bf16[20,1,45,720]{3,2,1,0:T(8,128)(2,1)S(1)}, bf16[20,1,45,720]{3,2,1,0:T(8,128)(2,1)}, u32[]{:S(2)}) copy-start(bf16[20,1,45,720]{3,2,1,0:T(8,128)(2,1)} %param.12) | copy-start | bytes 3888004
  6.5 13.2 %copy-start.7 = (s32[1,8]{1,0:T(1,128)S(1)}, s32[1,8]{1,0:T(1,128)}, u32[]{:S(2)}) copy-start(s32[1,8]{1,0:T(1,128)} %param.19) | copy-start | bytes 100
  6.5 13.2 %copy-start.5 = (f32[1,8,256]{2,1,0:T(8,128)S(1)}, f32[1,8,256]{2,1,0:T(8,128)}, u32[]{:S(2)}) copy-start(f32[1,8,256]{2,1,0:T(8,128)} %param.17) | copy-start | bytes 24580
  6.5 13.9 %copy-start.3 = (bf16[17]{0:T(256)(128)(2,1)S(1)}, bf16[17]{0:T(256)(128)(2,1)}, u32[]{:S(2)}) copy-start(bf16[17]{0:T(256)(128)(2,1)} %param.14) | copy-start | bytes 106
  6.5 14.6 %copy-start.4 = (bf16[17]{0:T(256)(128)(2,1)S(1)}, bf16[17]{0:T(256)(128)(2,1)}, u32[]{:S(2)}) copy-start(bf16[17]{0:T(256)(128)(2,1)} %param.15) | copy-start | bytes 106
  6.5 15.3 %copy-start.6 = (f32[1,8,256]{2,1,0:T(8,128)S(1)}, f32[1,8,256]{2,1,0:T(8,128)}, u32[]{:S(2)}) copy-start(f32[1,8,256]{2,1,0:T(8,128)} %param.16) | copy-start | bytes 24580
  8.1 32.6 %collective-permute-start.2 = (bf16[20,1,16,720]{3,2,0,1:T(8,128)(2,1)S(1)}, bf16[20,1,16,720]{3,2,0,1:T(8,128)(2,1)}, u32[]{:S(2)}, u32[]{:S(2)}) collective-permute-start(bf16[20,1,16,720]{3,2,0,1:T(8,128)(2,1)S(1)} %get-tuple-element.115), channel_id=1, source_target_pairs={{0,4},{4,8},{8,12},{12,16},{16,20},{20,24},{24,28},{28,0},{1,5},{5... | collective-permute-start | bytes 1382408 | tf_op jit(solution)/shard_map/ppermute | solution.py:14
  9.9 30.7 %collective-permute-start.3 = (bf16[20,1,16,720]{3,2,0,1:T(8,128)(2,1)S(1)}, bf16[20,1,16,720]{3,2,0,1:T(8,128)(2,1)}, u32[]{:S(2)}, u32[]{:S(2)}) collective-permute-start(bf16[20,1,16,720]{3,2,0,1:T(8,128)(2,1)S(1)} %get-tuple-element.116), channel_id=1, source_target_pairs={{4,0},{8,4},{12,8},{16,12},{20,16},{24,20},{28,24},{0,28},{5,1},{9... | collective-permute-start | bytes 1382408 | tf_op jit(solution)/shard_map/ppermute | solution.py:17
  11.2 12.0 %all-to-all-start = ((s32[1,8,256]{2,0,1:T(1,128)}), s32[1,8,256]{2,0,1:T(1,128)S(1)}, u32[]{:S(2)}, u32[]{:S(2)}) async-start(s32[1,8,256]{2,0,1:T(1,128)} %copy.48), calls=%async_computation | async-start | bytes 16384 | tf_op jit(solution)/shard_map/all_to_all | solution.py:136
  18.3 109.7 %collective-permute-start = (bf16[20,1,16,720]{3,2,0,1:T(8,128)(2,1)}, bf16[20,1,16,720]{3,2,0,1:T(8,128)(2,1)}, u32[]{:S(2)}, u32[]{:S(2)}) collective-permute-start(bf16[20,1,16,720]{3,2,0,1:T(8,128)(2,1)} %get-tuple-element.117), channel_id=1, source_target_pairs={{0,4},{4,8},{8,12},{12,16},{16,20},{20,24},{24,28},{28,0},{1,5},{5... | collective-permute-start | bytes 1382408 | tf_op jit(solution)/shard_map/ppermute | solution.py:14
  19.8 108.2 %collective-permute-start.1 = (bf16[20,1,16,720]{3,2,0,1:T(8,128)(2,1)S(1)}, bf16[20,1,16,720]{3,2,0,1:T(8,128)(2,1)}, u32[]{:S(2)}, u32[]{:S(2)}) collective-permute-start(bf16[20,1,16,720]{3,2,0,1:T(8,128)(2,1)S(1)} %get-tuple-element.118), channel_id=1, source_target_pairs={{4,0},{8,4},{12,8},{16,12},{20,16},{24,20},{28,24},{0,28},{5,1},{9... | collective-permute-start | bytes 1382408 | tf_op jit(solution)/shard_map/ppermute | solution.py:17
  23.2 10.1 %all-to-all-start.1 = ((f32[1,8,256]{2,0,1:T(1,128)}), f32[1,8,256]{2,0,1:T(1,128)S(1)}, u32[]{:S(2)}, u32[]{:S(2)}) async-start(f32[1,8,256]{2,0,1:T(1,128)} %compare_select_fusion), calls=%async_computation.1 | async-start | bytes 16384 | tf_op jit(solution)/shard_map/all_to_all | solution.py:135
  33.4 7.2 %all-to-all-start.2 = ((f32[1,8,256]{2,0,1:T(1,128)}), f32[1,8,256]{2,0,1:T(1,128)S(1)}, u32[]{:S(2)}, u32[]{:S(2)}) async-start(f32[1,8,256]{2,0,1:T(1,128)} %copy.57), calls=%async_computation.2 | async-start | bytes 16384 | tf_op jit(solution)/shard_map/all_to_all | solution.py:134
  37.3 74.3 %all-reduce.4.cloned.1.call-start = ((), (), s32[]{:S(2)}) async-start(), calls=%async_computation.3 | async-start | bytes 294912 | tf_op jit(solution)/shard_map/psum | solution.py:145
  112.7 3.8 %copy-start.2 = (f32[45,720]{1,0:T(8,128)S(1)}, f32[45,720]{1,0:T(8,128)}, u32[]{:S(2)}) copy-start(f32[45,720]{1,0:T(8,128)} %custom-call) | copy-start | bytes 388804
  116.5 11.5 %copy-start.1 = (bf16[20,1,45,720]{3,2,1,0:T(8,128)(2,1)S(1)}, bf16[20,1,45,720]{3,2,1,0:T(8,128)(2,1)}, u32[]{:S(2)}) copy-start(bf16[20,1,45,720]{3,2,1,0:T(8,128)(2,1)} %param.13) | copy-start | bytes 3888004
  119.7 5.1 %collective-permute-start.4 = (f32[1,16,720]{2,1,0:T(8,128)S(1)}, f32[1,16,720]{2,1,0:T(8,128)S(1)}, u32[]{:S(2)}, u32[]{:S(2)}) collective-permute-start(f32[1,16,720]{2,1,0:T(8,128)S(1)} %get-tuple-element.119), channel_id=1, source_target_pairs={{0,4},{4,8},{8,12},{12,16},{16,20},{20,24},{24,28},{28,0},{1,5},{5... | collective-permute-start | bytes 138248 | tf_op jit(solution)/shard_map/ppermute | solution.py:14
  123.5 4.4 %collective-permute-start.5 = (f32[1,16,720]{2,1,0:T(8,128)S(1)}, f32[1,16,720]{2,1,0:T(8,128)S(1)}, u32[]{:S(2)}, u32[]{:S(2)}) collective-permute-start(f32[1,16,720]{2,1,0:T(8,128)S(1)} %get-tuple-element.120), channel_id=1, source_target_pairs={{4,0},{8,4},{12,8},{16,12},{20,16},{24,20},{28,24},{0,28},{5,1},{9... | collective-permute-start | bytes 138248 | tf_op jit(solution)/shard_map/ppermute | solution.py:17
Sparse Core Ops, SparseCore 0:
  79.0 32.5 all-reduce.3
where the time goes:
time: 178 us; the launch traced here: 177 us
  matrix products  54 us (30%)
  waiting for transfers between devices  46.7 us (26%)
  local copies, waits for them, and re-layouts  37 us (21%)
  starting transfers between devices  20.5 us (12%)
  between operations  13.7 us (8%)
  other arithmetic  4.93 us (3%)
    psum x1, waiting for transfers between devices, local(): increment = lax.psum(member_sum, 'mem')  32.7 us
    dot_general x2, matrix products, localize(): jnp.einsum('ij,mljk->mlik', band_lon, extended, preferred_element_type=jn...  24.4 us
    dot_general x2, matrix products, localize(): jnp.einsum('mlibk,kq->mlibq', windows, band_blocks, preferred_element_typ...  23 us
    dot_general x2, local copies, waits for them, and re-layouts, localize(): jnp.einsum('mlibk,kq->mlibq', windows, band_blocks, preferred_element_typ...  12.8 us
    reshape x2, local copies, waits for them, and re-layouts, localize(): return result.reshape(members_here, levels, lon_cells, lat_cells)  9.75 us
    ppermute x3, starting transfers between devices, extended_2(): lax.ppermute(lax.slice_in_dim(block, block.shape[dim] - width, None, axis...  7.17 us
    all_to_all x1, waiting for transfers between devices, local(): lax.all_to_all(weights, 'tile', split_axis=1, concat_axis=0, tiled=True)  5.65 us
    all_to_all x1, starting transfers between devices, local(): lax.all_to_all(cell_index, 'tile', split_axis=1, concat_axis=0, tiled=True)  4.92 us
  transfers between devices with their start and end apart: 10, of which 6 were waited for; matrix products, arithmetic and copies ran while one was open for 30% of the time, Pallas kernels for 0%

commit v1 on v0

--- a/solution.py
+++ b/solution.py
@@ -142,7 +142,7 @@
     col_index = cells_hit % lat_cells
     row_count = levels * lon_cells
     block_rows = math.gcd(observed.shape[0], 1024)
-    increment = lax.psum(member_sum, "mem")
+    increment = jnp.sum(lax.all_gather(member_sum, "mem"), axis=0)
     at_cells = pick_cells(increment.reshape(row_count, lat_cells), row_index, col_index, block_rows)
     misfit = weight_recv * (at_cells - observed)
     spread = spread_cells(misfit, row_index, col_index, row_count, lat_cells, block_rows)

time: 178 us -> 146 us (0.82)
  waiting for transfers between devices: 46.7 us -> 13.8 us
  between operations: 13.7 us -> 0.35 us
  blocking collectives: 0 us -> 13.1 us
    psum x1 -> x0, waiting for transfers between devices: 32.7 us -> none  [local(): increment = lax.psum(member_sum, 'mem')]
    all_gather x0 -> x1, blocking collectives: none -> 13.1 us  [local(): increment = jnp.sum(lax.all_gather(member_sum, 'mem'), axis=0)]
  transfers between devices with their start and end apart: 10 -> 9, of which waited for: 6 -> 5; matrix products, arithmetic and copies ran while one was open for 30% -> 35% of each run, Pallas kernels for 0% -> 0%
where the time goes in v1:
time: 146 us; the launch traced here: 144 us
  matrix products  53.7 us (37%)
  local copies, waits for them, and re-layouts  36.1 us (25%)
  starting transfers between devices  22.2 us (15%)
  waiting for transfers between devices  13.8 us (9%)
  blocking collectives  13.1 us (9%)
  other arithmetic  4.32 us (3%)
    dot_general x2, matrix products, localize(): jnp.einsum('ij,mljk->mlik', band_lon, extended, preferred_element_type=jn...  24.3 us
    dot_general x2, matrix products, localize(): jnp.einsum('mlibk,kq->mlibq', windows, band_blocks, preferred_element_typ...  22.9 us
    all_gather x1, blocking collectives, local(): increment = jnp.sum(lax.all_gather(member_sum, 'mem'), axis=0)  13.1 us
    dot_general x2, local copies, waits for them, and re-layouts, localize(): jnp.einsum('mlibk,kq->mlibq', windows, band_blocks, preferred_element_typ...  12.8 us
    reshape x2, local copies, waits for them, and re-layouts, localize(): return result.reshape(members_here, levels, lon_cells, lat_cells)  9.75 us
    ppermute x3, starting transfers between devices, extended_2(): lax.ppermute(lax.slice_in_dim(block, block.shape[dim] - width, None, axis...  8.94 us
    all_to_all x1, waiting for transfers between devices, local(): lax.all_to_all(weights, 'tile', split_axis=1, concat_axis=0, tiled=True)  5.66 us
    all_to_all x1, starting transfers between devices, local(): lax.all_to_all(cell_index, 'tile', split_axis=1, concat_axis=0, tiled=True)  4.92 us
  transfers between devices with their start and end apart: 9, of which 5 were waited for; matrix products, arithmetic and copies ran while one was open for 35% of the time, Pallas kernels for 0%

profile of v1, /device:TPU:11, one launch (start us, length us, event | category | flops | bytes accessed | tf_op | source)
XLA Modules:
  0.0 143.7 jit_solution(11387983166309792231)
XLA Ops:
  0.0 1.5 %fusion.166 = (bf16[20,1,16,720]{3,2,0,1:T(8,128)(2,1)S(1)}, bf16[20,1,16,720]{3,2,0,1:T(8,128)(2,1)S(1)}) fusion(bf16[20,1,45,720]{3,2,0,1:T(8,128)(2,1)} %bitcast.146), kind=kLoop, calls=%fused_computation.199 | loop fusion | bytes 1843200 | tf_op jit(solution)/shard_map/slice | solution.py:15
  1.5 1.8 %collective-permute-start.2 = (bf16[20,1,16,720]{3,2,0,1:T(8,128)(2,1)S(1)}, bf16[20,1,16,720]{3,2,0,1:T(8,128)(2,1)}, u32[]{:S(2)}, u32[]{:S(2)}) collective-permute-start(bf16[20,1,16,720]{3,2,0,1:T(8,128)(2,1)S(1)} %get-tuple-element.110), channel_id=1, source_target_pairs={{0,4},{4,8},{8,12},{12,16},{16,20},{20,24},{24,28},{28,0},{1,5},{5... | collective-permute-start | bytes 1382408 | tf_op jit(solution)/shard_map/ppermute | solution.py:14
  3.4 1.3 copy.62
  4.7 4.9 %all-to-all-start = ((s32[1,8,256]{2,0,1:T(1,128)}), s32[1,8,256]{2,0,1:T(1,128)S(1)}, u32[]{:S(2)}, u32[]{:S(2)}) async-start(s32[1,8,256]{2,0,1:T(1,128)} %copy.62), calls=%async_computation | async-start | bytes 16384 | tf_op jit(solution)/shard_map/all_to_all | solution.py:136
  9.6 2.2 %fusion.167 = (bf16[20,1,16,720]{3,2,0,1:T(8,128)(2,1)}, bf16[20,1,16,720]{3,2,0,1:T(8,128)(2,1)S(1)}) fusion(bf16[20,1,45,720]{3,2,0,1:T(8,128)(2,1)} %bitcast.148), kind=kLoop, calls=%fused_computation.200 | loop fusion | bytes 1843200 | tf_op jit(solution)/shard_map/slice | solution.py:15
  11.8 1.5 %collective-permute-start = (bf16[20,1,16,720]{3,2,0,1:T(8,128)(2,1)}, bf16[20,1,16,720]{3,2,0,1:T(8,128)(2,1)}, u32[]{:S(2)}, u32[]{:S(2)}) collective-permute-start(bf16[20,1,16,720]{3,2,0,1:T(8,128)(2,1)} %get-tuple-element.112), channel_id=1, source_target_pairs={{0,4},{4,8},{8,12},{12,16},{16,20},{20,24},{24,28},{28,0},{1,5},{5... | collective-permute-start | bytes 1382408 | tf_op jit(solution)/shard_map/ppermute | solution.py:14
  14.0 0.7 fusion.169
  16.7 4.4 %all-to-all-start.1 = ((f32[1,8,256]{2,0,1:T(1,128)}), f32[1,8,256]{2,0,1:T(1,128)S(1)}, u32[]{:S(2)}, u32[]{:S(2)}) async-start(f32[1,8,256]{2,0,1:T(1,128)} %compare_select_fusion), calls=%async_computation.1 | async-start | bytes 16384 | tf_op jit(solution)/shard_map/all_to_all | solution.py:135
  21.2 5.7 %all-to-all-done.1 = f32[1,8,256]{2,0,1:T(1,128)S(1)} async-done(((f32[1,8,256]{2,0,1:T(1,128)}), f32[1,8,256]{2,0,1:T(1,128)S(1)}, u32[]{:S(2)}, u32[]{:S(2)}) %all-to-all-start.1) | async-done | bytes 8224 | tf_op jit(solution)/shard_map/all_to_all | solution.py:135
  26.8 4.0 %all-to-all-start.2 = ((f32[1,8,256]{2,0,1:T(1,128)}), f32[1,8,256]{2,0,1:T(1,128)S(1)}, u32[]{:S(2)}, u32[]{:S(2)}) async-start(f32[1,8,256]{2,0,1:T(1,128)} %copy.71), calls=%async_computation.2 | async-start | bytes 16384 | tf_op jit(solution)/shard_map/all_to_all | solution.py:134
  31.0 3.0 %all-to-all-done.2 = f32[1,8,256]{2,0,1:T(1,128)S(1)} async-done(((f32[1,8,256]{2,0,1:T(1,128)}), f32[1,8,256]{2,0,1:T(1,128)S(1)}, u32[]{:S(2)}, u32[]{:S(2)}) %all-to-all-start.2) | async-done | bytes 8224 | tf_op jit(solution)/shard_map/all_to_all | solution.py:134
  34.0 12.1 %fusion.31 = bf16[20,1,45,720]{3,2,0,1:T(8,128)(2,1)S(1)} fusion(bf16[20,1,16,720]{3,2,0,1:T(8,128)(2,1)} %collective-permute-done.3, bf16[20,1,45,720]{3,2,0,1:T(8,128)(2,1)S(1)} %bitcast.147, bf16[20,1,16,720]{3,2,0,1:T(8,128)(2,1)} %collective-permute-done.2, f32[]{:T(128)} %bitcast.31, f32[]{:T(128)} %bitcast.30, f32[]{:T(128)} %bitcast.29, ...), kind=kOutput, calls=%fused_computation.44 | convolution fusion | flops 107279912 | bytes 3513668 | tf_op jit(solution)/shard_map/ij,mljk->mlik/dot_general | solution.py:46
  47.0 11.4 %fusion.25 = f32[20,45,5,144]{3,1,2,0:T(8,128)S(1)} fusion(f32[]{:T(128)} %bitcast.58, f32[]{:T(128)} %bitcast.57, f32[]{:T(128)} %bitcast.56, f32[]{:T(128)} %bitcast.55, f32[]{:T(128)} %bitcast.54, f32[]{:T(128)} %bitcast.53, f32[]{:T(128)} %bitcast.52, f32[]{:T(128)} %bitcast.51, f32[]{:T(128)} %bitcast.50, f32[]{:T(128)} %bitcast.49, f32[]{:T(128)} %bitcast.48, ...), kind=kOutput, calls=%fused_computation.38 | convolution fusion | flops 229439232 | bytes 4176772 | tf_op jit(solution)/shard_map/mlibk,kq->mlibq/dot_general | solution.py:59
  58.4 6.4 %copy.69 = f32[20,45,5,144]{3,2,1,0:T(8,128)} copy(f32[20,45,5,144]{3,1,2,0:T(8,128)S(1)} %fusion.25) | data formatting | bytes 5184000 | tf_op jit(solution)/shard_map/mlibk,kq->mlibq/dot_general | solution.py:59
  64.8 4.9 %reshape.137 = f32[20,1,45,720]{3,2,0,1:T(8,128)S(1)} reshape(f32[20,45,5,144]{3,2,1,0:T(8,128)} %copy.69) | data formatting | bytes 5184000 | tf_op jit(solution)/shard_map/reshape | solution.py:60
  69.7 1.7 %multiply_reduce_fusion = f32[45,720]{1,0:T(8,128)S(1)} fusion(f32[20,1,45,720]{3,2,0,1:T(8,128)S(1)} %reshape.137, bf16[20,1,45,720]{3,2,1,0:T(8,128)(2,1)} %param.13), kind=kLoop, calls=%fused_computation.22 | loop fusion | flops 1911600 | bytes 4017600 | tf_op jit(solution)/shard_map/reduce_sum | solution.py:129
  71.4 13.1 %all-gather.1 = f32[4,45,720]{2,1,0:T(8,128)S(1)} all-gather(f32[1,45,720]{2,1,0:T(8,128)S(1)} %bitcast.150), channel_id=2, replica_groups=mesh['tile'=8,'mem'=4] {'mem'}, dimensions={0}, use_global_device_ids=true | all-gather | bytes 648000 | tf_op jit(solution)/shard_map/all_gather | solution.py:145
  84.7 3.8 %while.21 = (s32[]{:T(128)}, f32[2,1024]{1,0:T(2,128)S(1)}, s32[2,1024]{1,0:T(2,128)S(1)}, s32[2,1024]{1,0:T(2,128)S(1)}, f32[720,45]{1,0:T(8,128)S(1)}, /*index=5*/s32[]{:T(128)}, s32[]{:T(128)}) while((s32[]{:T(128)}, f32[2,1024]{1,0:T(2,128)S(1)}, s32[2,1024]{1,0:T(2,128)S(1)}, s32[2,1024]{1,0:T(2,128)S(1)}, f32[720,45]{1,0:T(8,128)S(1)}, ...), condition=%wide.region_4.5_spmd, body=%wide.region_2.4_spmd.sunk | while | flops 399005696 | bytes 166549 | solution.py:83
  84.7 1.8 %fusion.179 = f32[1024]{0:T(1024)S(1)} fusion(f32[720,45]{1,0:T(8,128)S(1)} %get-tuple-element.240, s32[1024]{0:T(1024)S(1)} %bitcast.158, s32[1024]{0:T(1024)S(1)} %bitcast.159), kind=kOutput, calls=%fused_computation.4.clone.1 | convolution fusion | flops 399005696 | bytes 141888 | tf_op jit(solution)/shard_map/while/body/eval_jaxpr/dot_general | solution.py:75
  86.6 1.8 %fusion.179 = f32[1024]{0:T(1024)S(1)} fusion(f32[720,45]{1,0:T(8,128)S(1)} %get-tuple-element.240, s32[1024]{0:T(1024)S(1)} %bitcast.158, s32[1024]{0:T(1024)S(1)} %bitcast.159), kind=kOutput, calls=%fused_computation.4.clone.1 | convolution fusion | flops 399005696 | bytes 141888 | tf_op jit(solution)/shard_map/while/body/eval_jaxpr/dot_general | solution.py:75
  88.5 3.1 %while.22 = (s32[]{:T(128)}, f32[45,720]{1,0:T(8,128)S(1)}, s32[2,1024]{1,0:T(2,128)S(1)}, f32[2,1024]{1,0:T(2,128)S(1)}, s32[2,1024]{1,0:T(2,128)S(1)}, /*index=5*/s32[]{:T(128)}, s32[]{:T(128)}) while((s32[]{:T(128)}, f32[45,720]{1,0:T(8,128)S(1)}, s32[2,1024]{1,0:T(2,128)S(1)}, f32[2,1024]{1,0:T(2,128)S(1)}, ...), condition=%wide.region_6.7_spmd.clone, body=%wide.region_5.6_spmd.clone.sunk | while | flops 399025440 | bytes 296159 | solution.py:117
  88.6 1.5 %fusion.181 = f32[45,720]{1,0:T(8,128)S(1)} fusion(s32[1024]{0:T(1024)S(1)} %bitcast.156, f32[1024]{0:T(1024)S(1)} %bitcast.154, s32[1024]{0:T(1024)S(1)} %bitcast.157, f32[45,720]{1,0:T(8,128)S(1)} %get-tuple-element.251, pred[]{:T(512)S(6)} %compare.5), kind=kOutput, calls=%fused_computation.11.clone.1 | convolution fusion | flops 399025440 | bytes 271489 | tf_op jit(solution)/shard_map/while/body/eval_jaxpr/dot_general | solution.py:102
  90.2 1.5 %fusion.181 = f32[45,720]{1,0:T(8,128)S(1)} fusion(s32[1024]{0:T(1024)S(1)} %bitcast.156, f32[1024]{0:T(1024)S(1)} %bitcast.154, s32[1024]{0:T(1024)S(1)} %bitcast.157, f32[45,720]{1,0:T(8,128)S(1)} %get-tuple-element.251, pred[]{:T(512)S(6)} %compare.5), kind=kOutput, calls=%fused_computation.11.clone.1 | convolution fusion | flops 399025440 | bytes 271489 | tf_op jit(solution)/shard_map/while/body/eval_jaxpr/dot_general | solution.py:102
  91.7 5.6 %collective-permute-start.4 = (f32[1,16,720]{2,1,0:T(8,128)S(1)}, f32[1,16,720]{2,1,0:T(8,128)S(1)}, u32[]{:S(2)}, u32[]{:S(2)}) collective-permute-start(f32[1,16,720]{2,1,0:T(8,128)S(1)} %get-tuple-element.114), channel_id=1, source_target_pairs={{0,4},{4,8},{8,12},{12,16},{16,20},{20,24},{24,28},{28,0},{1,5},{5... | collective-permute-start | bytes 138248 | tf_op jit(solution)/shard_map/ppermute | solution.py:14
  97.3 1.2 collective-permute-done.4
  98.5 3.2 %collective-permute-done.5 = f32[1,16,720]{2,1,0:T(8,128)S(1)} collective-permute-done((f32[1,16,720]{2,1,0:T(8,128)S(1)}, f32[1,16,720]{2,1,0:T(8,128)S(1)}, u32[]{:S(2)}, u32[]{:S(2)}) %collective-permute-start.5) | collective-permute-done | bytes 46112 | tf_op jit(solution)/shard_map/ppermute | solution.py:17
  101.8 12.3 %fusion.30 = bf16[20,1,45,720]{3,2,0,1:T(8,128)(2,1)S(1)} fusion(bf16[20,16,720]{2,1,0:T(8,128)(2,1)} %bitcast.8, bf16[20,45,720]{2,1,0:T(8,128)(2,1)S(1)} %bitcast.149, bf16[20,16,720]{2,1,0:T(8,128)(2,1)} %bitcast.5, f32[77,720]{1,0:T(8,128)S(1)} %maximum_bitcast_fusion.6, f32[]{:T(128)} %bitcast.31, f32[]{:T(128)} %bitcast.30, f32[]{:T(128)} %bitcast.29, ...), kind=kOutput, calls=%fused_computation.43 | convolution fusion | flops 109497512 | bytes 3735428 | tf_op jit(solution)/shard_map/ij,mljk->mlik/dot_general | solution.py:46
  115.0 11.4 %fusion.23 = f32[20,45,5,144]{3,1,2,0:T(8,128)S(1)} fusion(f32[]{:T(128)} %bitcast.58, f32[]{:T(128)} %bitcast.57, f32[]{:T(128)} %bitcast.56, f32[]{:T(128)} %bitcast.55, f32[]{:T(128)} %bitcast.54, f32[]{:T(128)} %bitcast.53, f32[]{:T(128)} %bitcast.52, f32[]{:T(128)} %bitcast.51, f32[]{:T(128)} %bitcast.50, f32[]{:T(128)} %bitcast.49, f32[]{:T(128)} %bitcast.48, ...), kind=kOutput, calls=%fused_computation.36 | convolution fusion | flops 229439232 | bytes 4176772 | tf_op jit(solution)/shard_map/mlibk,kq->mlibq/dot_general | solution.py:59
  126.4 6.4 %copy.73 = f32[20,45,5,144]{3,2,1,0:T(8,128)} copy(f32[20,45,5,144]{3,1,2,0:T(8,128)S(1)} %fusion.23) | data formatting | bytes 5184000 | tf_op jit(solution)/shard_map/mlibk,kq->mlibq/dot_general | solution.py:59
  132.8 4.9 %reshape.141 = f32[20,1,45,720]{3,2,0,1:T(8,128)S(1)} reshape(f32[20,45,5,144]{3,2,1,0:T(8,128)} %copy.73) | data formatting | bytes 5184000 | tf_op jit(solution)/shard_map/reshape | solution.py:60
  137.7 1.7 %convert_add_fusion = f32[20,1,45,720]{3,2,0,1:T(8,128)S(1)} fusion(f32[20,1,45,720]{3,2,0,1:T(8,128)S(1)} %reshape.141, bf16[20,1,45,720]{3,2,1,0:T(8,128)(2,1)} %param.12), kind=kLoop, calls=%fused_computation.23 | loop fusion | flops 1296000 | bytes 6480000 | tf_op jit(solution)/shard_map/add | solution.py:153
  139.3 4.4 %copy.74 = f32[20,1,45,720]{3,1,2,0:T(1,128)} copy(f32[20,1,45,720]{3,2,0,1:T(8,128)S(1)} %convert_add_fusion) | data formatting | bytes 5184000 | tf_op jit(solution)/shard_map/add | solution.py:153
  (63 shorter events, 5.2 us)
Async XLA Ops:
  0.0 34.0 %copy-start = (bf16[20,1,45,720]{3,2,1,0:T(8,128)(2,1)S(1)}, bf16[20,1,45,720]{3,2,1,0:T(8,128)(2,1)}, u32[]{:S(2)}) copy-start(bf16[20,1,45,720]{3,2,1,0:T(8,128)(2,1)} %param.12) | copy-start | bytes 3888004
  0.0 13.2 %copy-start.3 = (bf16[17]{0:T(256)(128)(2,1)S(1)}, bf16[17]{0:T(256)(128)(2,1)}, u32[]{:S(2)}) copy-start(bf16[17]{0:T(256)(128)(2,1)} %param.14) | copy-start | bytes 106
  0.0 14.0 %copy-start.4 = (bf16[17]{0:T(256)(128)(2,1)S(1)}, bf16[17]{0:T(256)(128)(2,1)}, u32[]{:S(2)}) copy-start(bf16[17]{0:T(256)(128)(2,1)} %param.15) | copy-start | bytes 106
  0.0 14.7 %copy-start.7 = (s32[1,8]{1,0:T(1,128)S(1)}, s32[1,8]{1,0:T(1,128)}, u32[]{:S(2)}) copy-start(s32[1,8]{1,0:T(1,128)} %param.19) | copy-start | bytes 100
  0.0 14.7 %copy-start.5 = (f32[1,8,256]{2,1,0:T(8,128)S(1)}, f32[1,8,256]{2,1,0:T(8,128)}, u32[]{:S(2)}) copy-start(f32[1,8,256]{2,1,0:T(8,128)} %param.17) | copy-start | bytes 24580
  0.0 15.4 %copy-start.6 = (f32[1,8,256]{2,1,0:T(8,128)S(1)}, f32[1,8,256]{2,1,0:T(8,128)}, u32[]{:S(2)}) copy-start(f32[1,8,256]{2,1,0:T(8,128)} %param.16) | copy-start | bytes 24580
  1.5 32.4 %collective-permute-start.2 = (bf16[20,1,16,720]{3,2,0,1:T(8,128)(2,1)S(1)}, bf16[20,1,16,720]{3,2,0,1:T(8,128)(2,1)}, u32[]{:S(2)}, u32[]{:S(2)}) collective-permute-start(bf16[20,1,16,720]{3,2,0,1:T(8,128)(2,1)S(1)} %get-tuple-element.110), channel_id=1, source_target_pairs={{0,4},{4,8},{8,12},{12,16},{16,20},{20,24},{24,28},{28,0},{1,5},{5... | collective-permute-start | bytes 1382408 | tf_op jit(solution)/shard_map/ppermute | solution.py:14
  3.4 30.6 %collective-permute-start.3 = (bf16[20,1,16,720]{3,2,0,1:T(8,128)(2,1)S(1)}, bf16[20,1,16,720]{3,2,0,1:T(8,128)(2,1)}, u32[]{:S(2)}, u32[]{:S(2)}) collective-permute-start(bf16[20,1,16,720]{3,2,0,1:T(8,128)(2,1)S(1)} %get-tuple-element.111), channel_id=1, source_target_pairs={{4,0},{8,4},{12,8},{16,12},{20,16},{24,20},{28,24},{0,28},{5,1},{9... | collective-permute-start | bytes 1382408 | tf_op jit(solution)/shard_map/ppermute | solution.py:17
  4.7 12.0 %all-to-all-start = ((s32[1,8,256]{2,0,1:T(1,128)}), s32[1,8,256]{2,0,1:T(1,128)S(1)}, u32[]{:S(2)}, u32[]{:S(2)}) async-start(s32[1,8,256]{2,0,1:T(1,128)} %copy.62), calls=%async_computation | async-start | bytes 16384 | tf_op jit(solution)/shard_map/all_to_all | solution.py:136
  11.8 90.0 %collective-permute-start = (bf16[20,1,16,720]{3,2,0,1:T(8,128)(2,1)}, bf16[20,1,16,720]{3,2,0,1:T(8,128)(2,1)}, u32[]{:S(2)}, u32[]{:S(2)}) collective-permute-start(bf16[20,1,16,720]{3,2,0,1:T(8,128)(2,1)} %get-tuple-element.112), channel_id=1, source_target_pairs={{0,4},{4,8},{8,12},{12,16},{16,20},{20,24},{24,28},{28,0},{1,5},{5... | collective-permute-start | bytes 1382408 | tf_op jit(solution)/shard_map/ppermute | solution.py:14
  13.2 88.5 %collective-permute-start.1 = (bf16[20,1,16,720]{3,2,0,1:T(8,128)(2,1)S(1)}, bf16[20,1,16,720]{3,2,0,1:T(8,128)(2,1)}, u32[]{:S(2)}, u32[]{:S(2)}) collective-permute-start(bf16[20,1,16,720]{3,2,0,1:T(8,128)(2,1)S(1)} %get-tuple-element.113), channel_id=1, source_target_pairs={{4,0},{8,4},{12,8},{16,12},{20,16},{24,20},{28,24},{0,28},{5,1},{9... | collective-permute-start | bytes 1382408 | tf_op jit(solution)/shard_map/ppermute | solution.py:17
  16.7 10.1 %all-to-all-start.1 = ((f32[1,8,256]{2,0,1:T(1,128)}), f32[1,8,256]{2,0,1:T(1,128)S(1)}, u32[]{:S(2)}, u32[]{:S(2)}) async-start(f32[1,8,256]{2,0,1:T(1,128)} %compare_select_fusion), calls=%async_computation.1 | async-start | bytes 16384 | tf_op jit(solution)/shard_map/all_to_all | solution.py:135
  26.8 7.1 %all-to-all-start.2 = ((f32[1,8,256]{2,0,1:T(1,128)}), f32[1,8,256]{2,0,1:T(1,128)S(1)}, u32[]{:S(2)}, u32[]{:S(2)}) async-start(f32[1,8,256]{2,0,1:T(1,128)} %copy.71), calls=%async_computation.2 | async-start | bytes 16384 | tf_op jit(solution)/shard_map/all_to_all | solution.py:134
  84.7 3.8 %copy-start.2 = (f32[45,720]{1,0:T(8,128)S(1)}, f32[45,720]{1,0:T(8,128)}, u32[]{:S(2)}) copy-start(f32[45,720]{1,0:T(8,128)} %custom-call) | copy-start | bytes 388804
  88.5 13.3 %copy-start.1 = (bf16[20,1,45,720]{3,2,1,0:T(8,128)(2,1)S(1)}, bf16[20,1,45,720]{3,2,1,0:T(8,128)(2,1)}, u32[]{:S(2)}) copy-start(bf16[20,1,45,720]{3,2,1,0:T(8,128)(2,1)} %param.13) | copy-start | bytes 3888004
  91.7 6.8 %collective-permute-start.4 = (f32[1,16,720]{2,1,0:T(8,128)S(1)}, f32[1,16,720]{2,1,0:T(8,128)S(1)}, u32[]{:S(2)}, u32[]{:S(2)}) collective-permute-start(f32[1,16,720]{2,1,0:T(8,128)S(1)} %get-tuple-element.114), channel_id=1, source_target_pairs={{0,4},{4,8},{8,12},{12,16},{16,20},{20,24},{24,28},{28,0},{1,5},{5... | collective-permute-start | bytes 138248 | tf_op jit(solution)/shard_map/ppermute | solution.py:14
  97.3 4.4 %collective-permute-start.5 = (f32[1,16,720]{2,1,0:T(8,128)S(1)}, f32[1,16,720]{2,1,0:T(8,128)S(1)}, u32[]{:S(2)}, u32[]{:S(2)}) collective-permute-start(f32[1,16,720]{2,1,0:T(8,128)S(1)} %get-tuple-element.115), channel_id=1, source_target_pairs={{4,0},{8,4},{12,8},{16,12},{20,16},{24,20},{28,24},{0,28},{5,1},{9... | collective-permute-start | bytes 138248 | tf_op jit(solution)/shard_map/ppermute | solution.py:17
